TPU v7x, 256 devices: a whole 4x4x8 slice. The times are simulated.
256 devices in a mesh: section: 2 (over core), patch: 4 (over y), req: 32 (over z, x).
Axes of the slice: x: 4, y: 4, z: 8, core: 2. Of those that a mesh axis runs over, the one named last changes fastest.
Arguments:
- hidden: bfloat16 [64, 1024, 1536], P('req', 'patch'), may hold values from -6 to 6
- w_qkv: bfloat16 [2, 1536, 2304], P('section', ('patch', 'req')), may hold values from -0.15625 to 0.15625
- w_out: bfloat16 [2, 768, 1536], P('section', ('patch', 'req')), may hold values from -0.21875 to 0.21875
- modulation: float32 [2, 64, 3, 1536], P('section', 'req'), may hold values from -3 to 3
- text_kv: bfloat16 [2, 64, 160, 1536], P('section', 'req'), may hold values from -1000 to 1000
- text_lengths: int32 [64], P('req'), may hold values from 77 to 154, as said below
- stale_kv: bfloat16 [2, 64, 1024, 1536], P('section', 'req', 'patch'), may hold values from -48 to 48
- held_hidden: bfloat16 [2, 64, 96, 1536], P('section', 'req', 'patch'), may hold values from -6 to 6
- recompute_rows: int32 [2, 64, 96], P('section', 'req', 'patch'), may hold values from 0 to 255, as said below
- coefficients: float32 [64, 2], P('req'), may hold values from 0.5 to 1.5
Outputs:
- latents: float32 [64, 1024, 1536], P('req', 'patch', 'section')
- cache: bfloat16 [2, 64, 1024, 1536], P('section', 'req', 'patch')
Inputs may be any that keep to these rules, and one draw needn't show every extreme that they name: `text_lengths`: some request has exactly 154 text tokens and some exactly 77. `recompute_rows`: the row numbers listed for one layer, request and patch are distinct.
All inputs are finite; a program needn't handle non-finite values.
Results may differ from a plain program's by a relative error of at most 0.025.
Values may be sent and summed in bfloat16 or wider, within the bound.
No kernel may reach another device: no remote copies, remote signals or barrier semaphores. Data moves between devices by JAX's collectives and lax.ppermute only.
A program may use at most 128 MiB of HBM per device.

v0:
```python
import jax
import jax.numpy as jnp
from jax import lax
from jax.sharding import PartitionSpec as P

HEADS = 12
norm_eps = 1e-06
score_scale = 0.125


def shifted(block, axis, distance):
    devices = range(lax.axis_size(axis))
    route = [(i - distance, i) for i in devices if i - distance in devices]
    return lax.ppermute(block, axis, route)


def modulate(row_block, shift_row, scale_row):
    values = row_block.astype(jnp.float32)
    centre = values - jnp.mean(values, axis=-1, keepdims=True)
    spread = jnp.mean(centre * centre, axis=-1, keepdims=True)
    return (centre * lax.rsqrt(spread + norm_eps) * (1.0 + scale_row) + shift_row).astype(
        jnp.bfloat16
    )


def attend(queries, key_rows, value_rows, usable):
    row_count = queries.shape[0]
    feature_count = queries.shape[1]
    query_heads = queries.reshape(row_count, HEADS, feature_count // HEADS)
    key_heads = key_rows.reshape(key_rows.shape[0], HEADS, feature_count // HEADS)
    value_heads = value_rows.reshape(value_rows.shape[0], HEADS, feature_count // HEADS)
    scores = (
        jnp.einsum("qhd,khd->hqk", query_heads, key_heads, preferred_element_type=jnp.float32)
        * score_scale
    )
    scores = jnp.where(usable[None, None, :], scores, -1e30)
    row_max = jnp.max(scores, axis=-1, keepdims=True)
    exp_scores = jnp.exp(scores - row_max)
    soft_weights = (exp_scores / jnp.sum(exp_scores, axis=-1, keepdims=True)).astype(jnp.bfloat16)
    attended = jnp.einsum(
        "hqk,khd->qhd", soft_weights, value_heads, preferred_element_type=jnp.float32
    )
    return attended.reshape(row_count, feature_count).astype(jnp.bfloat16)


def body(
    hidden,
    w_qkv,
    w_out,
    modulation,
    text_kv,
    text_lengths,
    stale_kv,
    held_hidden,
    recompute_rows,
    coefficients,
):
    full_qkv, full_out = (
        lax.all_gather(w_qkv[0], ("patch", "req"), axis=0, tiled=True),
        lax.all_gather(w_out[0], ("patch", "req"), axis=0, tiled=True),
    )
    section_index = lax.axis_index("section")
    patch_index = lax.axis_index("patch")
    request_count = hidden.shape[0]
    patch_rows = hidden.shape[1]
    model_width = hidden.shape[2]
    head_width = full_out.shape[0]
    text_slots = text_kv.shape[2]

    def process(layer_input, slot_index):
        mod_rows = lax.dynamic_index_in_dim(modulation[0], slot_index, 0, keepdims=False)
        text_rows = lax.dynamic_index_in_dim(text_kv[0], slot_index, 0, keepdims=False)
        text_count = lax.dynamic_index_in_dim(text_lengths, slot_index, 0, keepdims=False)
        stale_block = lax.dynamic_index_in_dim(stale_kv[0], slot_index, 0, keepdims=False)
        held_rows = lax.dynamic_index_in_dim(held_hidden[0], slot_index, 0, keepdims=False)
        redo_index = lax.dynamic_index_in_dim(recompute_rows[0], slot_index, 0, keepdims=False)
        held_norm = modulate(held_rows, mod_rows[0], mod_rows[1])
        redone = jnp.dot(
            held_norm, full_qkv[:, head_width:], preferred_element_type=jnp.float32
        ).astype(jnp.bfloat16)
        patched = stale_block.at[redo_index].set(redone)
        image_rows = lax.all_gather(patched, "patch", axis=0, tiled=True)
        normed = modulate(layer_input, mod_rows[0], mod_rows[1])
        projected = jnp.dot(normed, full_qkv, preferred_element_type=jnp.float32).astype(
            jnp.bfloat16
        )
        fresh_rows = projected[:, head_width:]
        image_rows = lax.dynamic_update_slice_in_dim(
            image_rows, fresh_rows, patch_index * patch_rows, 0
        )
        context = jnp.concatenate([text_rows, image_rows], axis=0)
        usable = jnp.concatenate(
            [jnp.arange(text_slots) < text_count, jnp.ones((image_rows.shape[0],), jnp.bool_)]
        )
        attended = attend(
            projected[:, :head_width], context[:, :head_width], context[:, head_width:], usable
        )
        update = jnp.dot(attended, full_out, preferred_element_type=jnp.float32)
        layer_out = (layer_input.astype(jnp.float32) + mod_rows[2] * update).astype(jnp.bfloat16)
        return (layer_out, fresh_rows)

    first_pass = [process(hidden[slot_number], slot_number) for slot_number in range(request_count)]
    first_out = jnp.stack([entry[0] for entry in first_pass])
    first_fresh = jnp.stack([entry[1] for entry in first_pass])
    received = shifted(first_out, "section", 1)
    second_pass = [
        process(received[slot_number], slot_number) for slot_number in range(request_count)
    ]
    second_out = jnp.stack([entry[0] for entry in second_pass])
    second_fresh = jnp.stack([entry[1] for entry in second_pass])
    fresh_all = jnp.where(section_index == 0, first_fresh, second_fresh)
    half_width = model_width // 2
    returned = shifted(second_out[:, :, :half_width], "section", -1)
    own_half = jnp.where(section_index == 0, returned, second_out[:, :, half_width:])
    source_half = lax.dynamic_slice_in_dim(hidden, section_index * half_width, half_width, 2)
    latents = coefficients[:, 0][:, None, None] * source_half.astype(jnp.float32) + coefficients[
        :, 1
    ][:, None, None] * own_half.astype(jnp.float32)
    return (latents, fresh_all[None])


def solution(mesh):
    return jax.shard_map(
        body,
        mesh=mesh,
        in_specs=(
            P("req", "patch", None),
            P("section", ("patch", "req"), None),
            P("section", ("patch", "req"), None),
            P("section", "req", None, None),
            P("section", "req", None, None),
            P("req"),
            P("section", "req", "patch", None),
            P("section", "req", "patch", None),
            P("section", "req", "patch"),
            P("req", None),
        ),
        out_specs=(P("req", "patch", "section"), P("section", "req", "patch", None)),
        check_vma=False,
    )
```

profile of v0, /device:TPU:1, one launch (start us, length us, event | category | flops | bytes accessed | tf_op | source)
XLA Modules:
  0.0 496.8 jit_solution(3415797970322674418)
XLA Ops:
  15.7 140.7 %all-gather.11.cloned.1.call-done = bf16[1,1536,2304]{2,0,1:T(2,128)(2,1)} async-done(((bf16[1,12,2304]{2,0,1:T(2,128)(2,1)}), bf16[1,1536,2304]{2,0,1:T(2,128)(2,1)}) %all-gather.11.cloned.1.call-update) | async-done | bytes 7077904 | tf_op jit(solution)/shard_map/all_gather | solution.py:59
  156.4 9.0 %copy.67 = bf16[1,1536,2304]{2,1,0:T(8,128)(2,1)} copy(bf16[1,1536,2304]{2,0,1:T(2,128)(2,1)} %all-gather.11.cloned.1.call-done) | data formatting | bytes 14155776
  180.5 91.4 %all-gather.13.cloned.1.call-done = bf16[1,768,1536]{2,0,1:T(2,128)(2,1)} async-done(((bf16[1,6,1536]{2,0,1:T(2,128)(2,1)}), bf16[1,768,1536]{2,0,1:T(2,128)(2,1)}) %all-gather.13.cloned.1.call-update) | async-done | bytes 2359312 | tf_op jit(solution)/shard_map/all_gather | solution.py:60
  275.0 5.2 %convolution_convert_fusion.3 = bf16[256,2304]{1,0:T(8,128)(2,1)S(1)} fusion(bf16[1536,2304]{1,0:T(8,128)(2,1)} %bitcast.210, f32[1536]{0:T(1024)S(1)} %get-tuple-element.16, f32[1536]{0:T(1024)S(1)} %get-tuple-element.17, f32[256]{0:T(256)S(1)} %add_rsqrt_fusion.3, f32[256]{0:T(256)S(1)} %broadcast_multiply_fusion.3, bf16[2,256,1536]{2,1,0:T(8,128)(2,1)S(1)} %copy-done.1), kind=kOutput, calls=%fused_computation.46 | convolution fusion | flops 1814888448 | bytes 9062400 | tf_op jit(solution)/shard_map/dot_general | solution.py:84
  283.9 5.7 %convolution_convert_fusion.2 = bf16[256,2304]{1,0:T(8,128)(2,1)S(1)} fusion(bf16[1536,2304]{1,0:T(8,128)(2,1)} %bitcast.211, f32[1536]{0:T(1024)S(1)} %get-tuple-element.18, f32[1536]{0:T(1024)S(1)} %get-tuple-element.19, f32[256]{0:T(256)S(1)} %add_rsqrt_fusion.2, f32[256]{0:T(256)S(1)} %broadcast_multiply_fusion.2, bf16[2,256,1536]{2,1,0:T(8,128)(2,1)} %param.10), kind=kOutput, calls=%fused_computation.45 | convolution fusion | flops 1814888448 | bytes 9058304 | tf_op jit(solution)/shard_map/dot_general | solution.py:84
  293.3 23.1 %all-gather.7.cloned.1.call-done = bf16[1024,1536]{1,0:T(8,128)(2,1)} async-done(((bf16[256,1536]{1,0:T(8,128)(2,1)}), bf16[1024,1536]{1,0:T(8,128)(2,1)}) %all-gather.7.cloned.1.call-update) | async-done | bytes 3145744 | tf_op jit(solution)/shard_map/all_gather | solution.py:82
  327.3 4.0 copy.51
  331.3 29.1 %all-gather.9.cloned.1.call-done = bf16[1024,1536]{1,0:T(8,128)(2,1)} async-done(((bf16[256,1536]{1,0:T(8,128)(2,1)}), bf16[1024,1536]{1,0:T(8,128)(2,1)}) %all-gather.9.cloned.1.call-update) | async-done | bytes 3145744 | tf_op jit(solution)/shard_map/all_gather | solution.py:82
  360.4 3.9 copy.72
  367.4 3.9 copy.57
  371.4 4.1 copy.55
  375.4 6.9 %fusion.178 = f32[12,256]{1,0:T(8,128)S(1)} fusion(pred[1184]{0:T(1024)(128)(4,1)S(1)} %concatenate.35, bf16[256,12,64]{0,2,1:T(8,128)(2,1)} %bitcast.232, bf16[1184,12,64]{0,2,1:T(8,128)(2,1)} %bitcast.216), kind=kOutput, calls=%fused_computation.243 | convolution fusion | flops 480117920 | bytes 2225312 | tf_op jit(solution)/shard_map/sub | solution.py:38
  382.3 9.5 %fusion.93 = bf16[12,64,256]{2,1,0:T(8,128)(2,1)} fusion(bf16[1184,12,64]{0,2,1:T(8,128)(2,1)} %bitcast.218, f32[12,256]{1,0:T(8,128)S(1)} %fusion.178, pred[1184]{0:T(1024)(128)(4,1)S(1)} %concatenate.35, bf16[256,12,64]{0,2,1:T(8,128)(2,1)} %bitcast.233, bf16[1184,12,64]{0,2,1:T(8,128)(2,1)} %bitcast.217), kind=kOutput, calls=%fused_computation.131 | convolution fusion | flops 949522560 | bytes 4437152 | tf_op jit(solution)/shard_map/hqk,khd->qhd/dot_general | solution.py:40
  391.8 7.1 %fusion.177 = f32[12,256]{1,0:T(8,128)S(1)} fusion(pred[1184]{0:T(1024)(128)(4,1)S(1)} %concatenate.37, bf16[256,12,64]{0,2,1:T(8,128)(2,1)} %bitcast.234, bf16[1184,12,64]{0,2,1:T(8,128)(2,1)} %bitcast.223), kind=kOutput, calls=%fused_computation.242 | convolution fusion | flops 480117920 | bytes 2225312 | tf_op jit(solution)/shard_map/sub | solution.py:38
  398.9 9.4 %fusion.92 = bf16[12,64,256]{2,1,0:T(8,128)(2,1)} fusion(bf16[1184,12,64]{0,2,1:T(8,128)(2,1)} %bitcast.227, f32[12,256]{1,0:T(8,128)S(1)} %fusion.177, pred[1184]{0:T(1024)(128)(4,1)S(1)} %concatenate.37, bf16[256,12,64]{0,2,1:T(8,128)(2,1)} %bitcast.235, bf16[1184,12,64]{0,2,1:T(8,128)(2,1)} %bitcast.224), kind=kOutput, calls=%fused_computation.130 | convolution fusion | flops 949522560 | bytes 4437152 | tf_op jit(solution)/shard_map/hqk,khd->qhd/dot_general | solution.py:40
  414.3 4.0 collective-permute-done
  429.5 4.0 copy.63
  433.7 4.1 copy.61
  437.7 4.0 copy.60
  441.9 4.1 copy.58
  446.0 6.7 %fusion.180 = f32[12,256]{1,0:T(8,128)S(1)} fusion(pred[1184]{0:T(1024)(128)(4,1)S(1)} %copy-done.30, bf16[256,12,64]{0,2,1:T(8,128)(2,1)S(1)} %bitcast.238, bf16[1184,12,64]{0,2,1:T(8,128)(2,1)} %bitcast.221), kind=kOutput, calls=%fused_computation.245 | convolution fusion | flops 480117920 | bytes 2225312 | tf_op jit(solution)/shard_map/sub | solution.py:38
  452.7 8.7 %fusion.90 = bf16[12,64,256]{2,1,0:T(8,128)(2,1)S(1)} fusion(bf16[1184,12,64]{0,2,1:T(8,128)(2,1)} %bitcast.225, f32[12,256]{1,0:T(8,128)S(1)} %fusion.180, pred[1184]{0:T(1024)(128)(4,1)S(1)} %copy-done.30, bf16[256,12,64]{0,2,1:T(8,128)(2,1)} %bitcast.239, bf16[1184,12,64]{0,2,1:T(8,128)(2,1)} %bitcast.222), kind=kOutput, calls=%fused_computation.128 | convolution fusion | flops 949522560 | bytes 4437152 | tf_op jit(solution)/shard_map/hqk,khd->qhd/dot_general | solution.py:40
  461.4 7.0 %fusion.179 = f32[12,256]{1,0:T(8,128)S(1)} fusion(pred[1184]{0:T(1024)(128)(4,1)S(1)} %copy-done.28, bf16[256,12,64]{0,2,1:T(8,128)(2,1)S(1)} %bitcast.236, bf16[1184,12,64]{0,2,1:T(8,128)(2,1)} %bitcast.219), kind=kOutput, calls=%fused_computation.244 | convolution fusion | flops 480117920 | bytes 2225312 | tf_op jit(solution)/shard_map/sub | solution.py:38
  468.4 9.3 %fusion.91 = bf16[12,64,256]{2,1,0:T(8,128)(2,1)} fusion(bf16[1184,12,64]{0,2,1:T(8,128)(2,1)} %bitcast.226, f32[12,256]{1,0:T(8,128)S(1)} %fusion.179, pred[1184]{0:T(1024)(128)(4,1)S(1)} %copy-done.28, bf16[256,12,64]{0,2,1:T(8,128)(2,1)S(1)} %bitcast.237, bf16[1184,12,64]{0,2,1:T(8,128)(2,1)} %bitcast.220), kind=kOutput, calls=%fused_computation.129 | convolution fusion | flops 949522560 | bytes 4437152 | tf_op jit(solution)/shard_map/hqk,khd->qhd/dot_general | solution.py:40
  (144 shorter events, 77.5 us)
Async XLA Ops:
  7.2 149.3 %all-gather.11.cloned.1.call-start = ((), (), s32[]{:S(2)}) async-start(), calls=%async_computation.2 | async-start | bytes 14266368 | tf_op jit(solution)/shard_map/all_gather | solution.py:59
  8.8 263.1 %all-gather.13.cloned.1.call-start = ((), (), s32[]{:S(2)}) async-start(), calls=%async_computation.3 | async-start | bytes 4755456 | tf_op jit(solution)/shard_map/all_gather | solution.py:60
  10.3 306.1 %all-gather.7.cloned.1.call-start = ((), (), s32[]{:S(2)}) async-start(), calls=%async_computation | async-start | bytes 3932160 | tf_op jit(solution)/shard_map/all_gather | solution.py:82
  15.7 149.7 %copy-start.23 = (bf16[1,2,24,1536]{3,2,1,0:T(8,128)(2,1)S(1)}, bf16[1,2,24,1536]{3,2,1,0:T(8,128)(2,1)}, u32[]{:S(2)}) copy-start(bf16[1,2,24,1536]{3,2,1,0:T(8,128)(2,1)} %param.17) | copy-start | bytes 442372
  170.6 189.7 %all-gather.9.cloned.1.call-start = ((), (), s32[]{:S(2)}) async-start(), calls=%async_computation.1 | async-start | bytes 3932160 | tf_op jit(solution)/shard_map/all_gather | solution.py:82
  173.9 4.5 copy-start
  177.8 204.5 %copy-start.27 = (pred[1184]{0:T(1024)(128)(4,1)}, pred[1184]{0:T(1024)(128)(4,1)S(1)}, u32[]{:S(2)}) copy-start(pred[1184]{0:T(1024)(128)(4,1)S(1)} %concatenate.35) | copy-start | bytes 3556
  178.4 220.5 %copy-start.29 = (pred[1184]{0:T(1024)(128)(4,1)}, pred[1184]{0:T(1024)(128)(4,1)S(1)}, u32[]{:S(2)}) copy-start(pred[1184]{0:T(1024)(128)(4,1)S(1)} %concatenate.37) | copy-start | bytes 3556
  360.4 3.9 copy-start.20
  408.3 10.9 %slice-start = ((s8[7077888]{0:T(1024)(128)(4,1)}), s8[4194304]{0:T(1024)(128)(4,1)S(1)}, s32[]{:S(2)}) async-start(s8[7077888]{0:T(1024)(128)(4,1)} %bitcast.212), calls=%async_computation.4 | async-start | bytes 8388608
  410.5 8.7 %slice-start.1 = ((s8[7077888]{0:T(1024)(128)(4,1)}), s8[2883584]{0:T(1024)(128)(4,1)S(1)}, s32[]{:S(2)}) async-start(s8[7077888]{0:T(1024)(128)(4,1)} %bitcast.212), calls=%async_computation.5 | async-start | bytes 5767168
  413.0 5.3 %collective-permute-start = (bf16[2,256,1536]{2,1,0:T(8,128)(2,1)S(1)}, bf16[2,256,1536]{2,1,0:T(8,128)(2,1)S(1)}, u32[]{:S(2)}, u32[]{:S(2)}) collective-permute-start(bf16[2,256,1536]{2,1,0:T(8,128)(2,1)S(1)} %pad_maximum_fusion.4), channel_id=1, source_target_pairs={{0,128},{1,129},{2,130},{3,131},{4,132},{5,133},{6,134},{7,135},{8... | collective-permute-start | bytes 4718600 | tf_op jit(solution)/shard_map/ppermute | solution.py:14
  418.3 4.4 copy-start.4
  424.9 4.6 copy-start.18
  429.5 4.0 slice-start.2
  433.7 12.3 %copy-start.25 = (bf16[256,768]{0,1:T(8,128)(2,1)}, bf16[256,768]{0,1:T(8,128)(2,1)S(1)}, u32[]{:S(2)}) copy-start(bf16[256,768]{0,1:T(8,128)(2,1)S(1)} %copy.62) | copy-start | bytes 1179652
  437.7 4.0 slice-start.3
  441.9 4.1 copy-start.30
  452.7 8.7 %copy-start.28 = (pred[1184]{0:T(1024)(128)(4,1)S(1)}, pred[1184]{0:T(1024)(128)(4,1)}, u32[]{:S(2)}) copy-start(pred[1184]{0:T(1024)(128)(4,1)} %copy-done.27) | copy-start | bytes 3556
  481.5 4.1 copy-start.26
  481.5 4.2 copy-start.14
  481.5 4.2 copy-start.15
  481.5 4.3 copy-start.16
  482.4 6.0 %collective-permute-start.1 = (bf16[2,256,768]{2,1,0:T(8,128)(2,1)}, bf16[2,256,768]{2,1,0:T(8,128)(2,1)}, u32[]{:S(2)}, u32[]{:S(2)}) collective-permute-start(bf16[2,256,768]{2,1,0:T(8,128)(2,1)} %fusion.94), channel_id=1, source_target_pairs={{128,0},{129,1},{130,2},{131,3},{132,4},{133,5},{134,6},{135,7},{1... | collective-permute-start | bytes 2359304 | tf_op jit(solution)/shard_map/ppermute | solution.py:14
  (18 other events, 39.6 us)
Sparse Core Ops, SparseCore 0:
  12.3 144.0 all-gather.10
  160.8 111.1 all-gather.12
  273.7 42.6 all-gather.6
  318.1 42.2 all-gather.8
where the time goes:
time: 502 us; the launch traced here: 497 us
  waiting for transfers between devices  288 us (57%)
  matrix products  93.5 us (19%)
  local copies, waits for them, and re-layouts  76.1 us (15%)
  other arithmetic  19.8 us (4%)
  between operations  14.6 us (3%)
    all_gather x1, waiting for transfers between devices, body(): lax.all_gather(w_qkv[0], ('patch', 'req'), axis=0, tiled=True)  141 us
    all_gather x1, waiting for transfers between devices, body(): lax.all_gather(w_out[0], ('patch', 'req'), axis=0, tiled=True)  91.4 us
    all_gather x2, waiting for transfers between devices, process(): image_rows = lax.all_gather(patched, 'patch', axis=0, tiled=True)  52.2 us
    dot_general x4, matrix products, attend(): jnp.einsum('hqk,khd->qhd', soft_weights, value_heads, preferred_element_t...  36.9 us
    unnamed x74, local copies, waits for them, and re-layouts  27.8 us
    sub x4, matrix products, attend(): exp_scores = jnp.exp(scores - row_max)  27.6 us
    slice x4, local copies, waits for them, and re-layouts, process(): context[:, head_width:]  16.2 us
    slice x4, local copies, waits for them, and re-layouts, process(): context[:, :head_width]  15.8 us
  transfers between devices with their start and end apart: 6, of which 5 were waited for; matrix products, arithmetic and copies ran while one was open for 13% of the time, Pallas kernels for 0%

commit v1 on v0

--- a/solution.py
+++ b/solution.py
@@ -6,6 +6,11 @@
 HEADS = 12
 norm_eps = 1e-06
 score_scale = 0.125
+
+
+def gather_from_all(value, axis, dim):
+    copies = jnp.concatenate([value] * lax.axis_size(axis), axis=dim)
+    return lax.all_to_all(copies, axis, dim, dim, tiled=True)
 
 
 def shifted(block, axis, distance):
@@ -79,7 +84,7 @@
             held_norm, full_qkv[:, head_width:], preferred_element_type=jnp.float32
         ).astype(jnp.bfloat16)
         patched = stale_block.at[redo_index].set(redone)
-        image_rows = lax.all_gather(patched, "patch", axis=0, tiled=True)
+        image_rows = gather_from_all(patched, "patch", 0)
         normed = modulate(layer_input, mod_rows[0], mod_rows[1])
         projected = jnp.dot(normed, full_qkv, preferred_element_type=jnp.float32).astype(
             jnp.bfloat16

time: 502 us -> 456 us (0.908)
  waiting for transfers between devices: 288 us -> 225 us
  other arithmetic: 19.8 us -> 29.1 us
  starting transfers between devices: 4.55 us -> 13.5 us
    all_gather x2 -> x0, waiting for transfers between devices: 52.2 us -> none  [process(): image_rows = lax.all_gather(patched, 'patch', axis=0, tiled=True)]
    all_gather x1, waiting for transfers between devices: 91.4 us -> 57.5 us  [body(): lax.all_gather(w_out[0], ('patch', 'req'), axis=0, tiled=True)]
    all_to_all x0 -> x2, waiting for transfers between devices: none -> 23.1 us  [gather_from_all(): return lax.all_to_all(copies, axis, dim, dim, tiled=True)]
    all_to_all x0 -> x2, starting transfers between devices: none -> 9.07 us  [gather_from_all(): return lax.all_to_all(copies, axis, dim, dim, tiled=True)]
    concatenate x0 -> x2, other arithmetic: none -> 5.34 us  [gather_from_all(): copies = jnp.concatenate([value] * lax.axis_size(axis), axis=dim)]
    unnamed x74 -> x76, local copies, waits for them, and re-layouts: 27.8 us -> 27.8 us
  transfers between devices with their start and end apart: 6 -> 6, of which waited for: 5 -> 4; matrix products, arithmetic and copies ran while one was open for 13% -> 16% of each run, Pallas kernels for 0% -> 0%
where the time goes in v1:
time: 456 us; the launch traced here: 450 us
  waiting for transfers between devices  225 us (49%)
  matrix products  93.1 us (20%)
  local copies, waits for them, and re-layouts  74.1 us (16%)
  other arithmetic  29.1 us (6%)
  between operations  14.9 us (3%)
  starting transfers between devices  13.5 us (3%)
    all_gather x1, waiting for transfers between devices, body(): lax.all_gather(w_qkv[0], ('patch', 'req'), axis=0, tiled=True)  138 us
    all_gather x1, waiting for transfers between devices, body(): lax.all_gather(w_out[0], ('patch', 'req'), axis=0, tiled=True)  57.5 us
    dot_general x4, matrix products, attend(): jnp.einsum('hqk,khd->qhd', soft_weights, value_heads, preferred_element_t...  36.9 us
    unnamed x76, local copies, waits for them, and re-layouts  27.8 us
    sub x4, matrix products, attend(): exp_scores = jnp.exp(scores - row_max)  27.6 us
    all_to_all x2, waiting for transfers between devices, gather_from_all(): return lax.all_to_all(copies, axis, dim, dim, tiled=True)  23.1 us
    slice x4, local copies, waits for them, and re-layouts, process(): context[:, head_width:]  16.2 us
    slice x4, local copies, waits for them, and re-layouts, process(): context[:, :head_width]  15.8 us
  transfers between devices with their start and end apart: 6, of which 4 were waited for; matrix products, arithmetic and copies ran while one was open for 16% of the time, Pallas kernels for 0%

profile of v1, /device:TPU:1, one launch (start us, length us, event | category | flops | bytes accessed | tf_op | source)
XLA Modules:
  0.0 449.9 jit_solution(6251086296014955691)
XLA Ops:
  18.2 138.2 %all-gather.5.cloned.1.call-done = bf16[1,1536,2304]{2,0,1:T(2,128)(2,1)} async-done(((bf16[1,12,2304]{2,0,1:T(2,128)(2,1)}), bf16[1,1536,2304]{2,0,1:T(2,128)(2,1)}) %all-gather.5.cloned.1.call-update) | async-done | bytes 7077904 | tf_op jit(solution)/shard_map/all_gather | solution.py:64
  156.4 9.0 %copy.67 = bf16[1,1536,2304]{2,1,0:T(8,128)(2,1)} copy(bf16[1,1536,2304]{2,0,1:T(2,128)(2,1)} %all-gather.5.cloned.1.call-done) | data formatting | bytes 14155776
  171.6 4.0 all-to-all-start
  188.9 23.1 %all-to-all-done = bf16[4,256,1536]{2,1,0:T(8,128)(2,1)S(1)} async-done(((bf16[4,256,1536]{2,1,0:T(8,128)(2,1)}), bf16[4,256,1536]{2,1,0:T(8,128)(2,1)S(1)}, u32[]{:S(2)}, u32[]{:S(2)}) %all-to-all-start) | async-done | bytes 3145760 | tf_op jit(solution)/shard_map/all_to_all | solution.py:13
  213.6 5.1 %all-to-all-start.1 = ((bf16[4,256,1536]{2,1,0:T(8,128)(2,1)}), bf16[4,256,1536]{2,1,0:T(8,128)(2,1)}, u32[]{:S(2)}, u32[]{:S(2)}) async-start(bf16[4,256,1536]{2,1,0:T(8,128)(2,1)} %bitcast.215), calls=%async_computation.1 | async-start | bytes 6291456 | tf_op jit(solution)/shard_map/all_to_all | solution.py:13
  218.7 57.5 %all-gather.7.cloned.1.call-done = bf16[1,768,1536]{2,0,1:T(2,128)(2,1)} async-done(((bf16[1,6,1536]{2,0,1:T(2,128)(2,1)}), bf16[1,768,1536]{2,0,1:T(2,128)(2,1)}) %all-gather.7.cloned.1.call-update) | async-done | bytes 2359312 | tf_op jit(solution)/shard_map/all_gather | solution.py:65
  279.2 5.2 %convolution_convert_fusion.3 = bf16[256,2304]{1,0:T(8,128)(2,1)S(1)} fusion(bf16[1536,2304]{1,0:T(8,128)(2,1)} %bitcast.218, f32[1536]{0:T(1024)S(1)} %get-tuple-element.16, f32[1536]{0:T(1024)S(1)} %get-tuple-element.17, f32[256]{0:T(256)S(1)} %add_rsqrt_fusion.3, f32[256]{0:T(256)S(1)} %broadcast_multiply_fusion.3, bf16[2,256,1536]{2,1,0:T(8,128)(2,1)S(1)} %copy-done.2), kind=kOutput, calls=%fused_computation.46 | convolution fusion | flops 1814888448 | bytes 9062400 | tf_op jit(solution)/shard_map/dot_general | solution.py:89
  286.4 5.4 %convolution_convert_fusion.2 = bf16[256,2304]{1,0:T(8,128)(2,1)S(1)} fusion(bf16[1536,2304]{1,0:T(8,128)(2,1)} %bitcast.219, f32[1536]{0:T(1024)S(1)} %get-tuple-element.18, f32[1536]{0:T(1024)S(1)} %get-tuple-element.19, f32[256]{0:T(256)S(1)} %add_rsqrt_fusion.2, f32[256]{0:T(256)S(1)} %broadcast_multiply_fusion.2, bf16[2,256,1536]{2,1,0:T(8,128)(2,1)} %param.10), kind=kOutput, calls=%fused_computation.45 | convolution fusion | flops 1814888448 | bytes 9058304 | tf_op jit(solution)/shard_map/dot_general | solution.py:89
  304.7 3.9 copy.51
  313.8 3.9 pad_maximum_fusion.3
  321.7 4.1 copy.55
  325.8 6.9 %fusion.178 = f32[12,256]{1,0:T(8,128)S(1)} fusion(pred[1184]{0:T(1024)(128)(4,1)S(1)} %concatenate.44, bf16[256,12,64]{0,2,1:T(8,128)(2,1)} %bitcast.240, bf16[1184,12,64]{0,2,1:T(8,128)(2,1)} %bitcast.224), kind=kOutput, calls=%fused_computation.245 | convolution fusion | flops 480117920 | bytes 2225312 | tf_op jit(solution)/shard_map/sub | solution.py:43
  332.6 9.4 %fusion.93 = bf16[12,64,256]{2,1,0:T(8,128)(2,1)} fusion(bf16[1184,12,64]{0,2,1:T(8,128)(2,1)} %bitcast.226, f32[12,256]{1,0:T(8,128)S(1)} %fusion.178, pred[1184]{0:T(1024)(128)(4,1)S(1)} %concatenate.44, bf16[256,12,64]{0,2,1:T(8,128)(2,1)} %bitcast.241, bf16[1184,12,64]{0,2,1:T(8,128)(2,1)} %bitcast.225), kind=kOutput, calls=%fused_computation.133 | convolution fusion | flops 949522560 | bytes 4437152 | tf_op jit(solution)/shard_map/hqk,khd->qhd/dot_general | solution.py:45
  342.1 7.1 %fusion.177 = f32[12,256]{1,0:T(8,128)S(1)} fusion(pred[1184]{0:T(1024)(128)(4,1)S(1)} %concatenate.47, bf16[256,12,64]{0,2,1:T(8,128)(2,1)} %bitcast.242, bf16[1184,12,64]{0,2,1:T(8,128)(2,1)} %bitcast.231), kind=kOutput, calls=%fused_computation.244 | convolution fusion | flops 480117920 | bytes 2225312 | tf_op jit(solution)/shard_map/sub | solution.py:43
  349.2 9.5 %fusion.92 = bf16[12,64,256]{2,1,0:T(8,128)(2,1)} fusion(bf16[1184,12,64]{0,2,1:T(8,128)(2,1)} %bitcast.235, f32[12,256]{1,0:T(8,128)S(1)} %fusion.177, pred[1184]{0:T(1024)(128)(4,1)S(1)} %concatenate.47, bf16[256,12,64]{0,2,1:T(8,128)(2,1)} %bitcast.243, bf16[1184,12,64]{0,2,1:T(8,128)(2,1)} %bitcast.232), kind=kOutput, calls=%fused_computation.132 | convolution fusion | flops 949522560 | bytes 4437152 | tf_op jit(solution)/shard_map/hqk,khd->qhd/dot_general | solution.py:45
  364.7 6.5 %collective-permute-done = bf16[2,256,1536]{2,1,0:T(8,128)(2,1)S(1)} collective-permute-done((bf16[2,256,1536]{2,1,0:T(8,128)(2,1)S(1)}, bf16[2,256,1536]{2,1,0:T(8,128)(2,1)S(1)}, u32[]{:S(2)}, u32[]{:S(2)}) %collective-permute-start) | collective-permute-done | bytes 1572896 | tf_op jit(solution)/shard_map/ppermute | solution.py:19
  382.3 4.0 copy.63
  386.5 4.1 copy.61
  390.6 4.0 copy.60
  394.7 4.1 copy.58
  398.8 6.7 %fusion.180 = f32[12,256]{1,0:T(8,128)S(1)} fusion(pred[1184]{0:T(1024)(128)(4,1)S(1)} %copy-done.31, bf16[256,12,64]{0,2,1:T(8,128)(2,1)S(1)} %bitcast.246, bf16[1184,12,64]{0,2,1:T(8,128)(2,1)} %bitcast.229), kind=kOutput, calls=%fused_computation.247 | convolution fusion | flops 480117920 | bytes 2225312 | tf_op jit(solution)/shard_map/sub | solution.py:43
  405.5 8.7 %fusion.90 = bf16[12,64,256]{2,1,0:T(8,128)(2,1)S(1)} fusion(bf16[1184,12,64]{0,2,1:T(8,128)(2,1)} %bitcast.233, f32[12,256]{1,0:T(8,128)S(1)} %fusion.180, pred[1184]{0:T(1024)(128)(4,1)S(1)} %copy-done.31, bf16[256,12,64]{0,2,1:T(8,128)(2,1)} %bitcast.247, bf16[1184,12,64]{0,2,1:T(8,128)(2,1)} %bitcast.230), kind=kOutput, calls=%fused_computation.130 | convolution fusion | flops 949522560 | bytes 4437152 | tf_op jit(solution)/shard_map/hqk,khd->qhd/dot_general | solution.py:45
  414.3 7.0 %fusion.179 = f32[12,256]{1,0:T(8,128)S(1)} fusion(pred[1184]{0:T(1024)(128)(4,1)S(1)} %copy-done.29, bf16[256,12,64]{0,2,1:T(8,128)(2,1)S(1)} %bitcast.244, bf16[1184,12,64]{0,2,1:T(8,128)(2,1)} %bitcast.227), kind=kOutput, calls=%fused_computation.246 | convolution fusion | flops 480117920 | bytes 2225312 | tf_op jit(solution)/shard_map/sub | solution.py:43
  421.2 9.3 %fusion.91 = bf16[12,64,256]{2,1,0:T(8,128)(2,1)} fusion(bf16[1184,12,64]{0,2,1:T(8,128)(2,1)} %bitcast.234, f32[12,256]{1,0:T(8,128)S(1)} %fusion.179, pred[1184]{0:T(1024)(128)(4,1)S(1)} %copy-done.29, bf16[256,12,64]{0,2,1:T(8,128)(2,1)S(1)} %bitcast.245, bf16[1184,12,64]{0,2,1:T(8,128)(2,1)} %bitcast.228), kind=kOutput, calls=%fused_computation.131 | convolution fusion | flops 949522560 | bytes 4437152 | tf_op jit(solution)/shard_map/hqk,khd->qhd/dot_general | solution.py:45
  (146 shorter events, 88.6 us)
Async XLA Ops:
  7.2 10.0 %copy-start.32 = (s32[1,2,24]{2,1,0:T(2,128)S(1)}, s32[1,2,24]{2,1,0:T(2,128)}, u32[]{:S(2)}) copy-start(s32[1,2,24]{2,1,0:T(2,128)} %param.18) | copy-start | bytes 580
  7.2 10.1 %copy-start.16 = (bf16[1,2,256,1536]{3,2,1,0:T(8,128)(2,1)S(1)}, bf16[1,2,256,1536]{3,2,1,0:T(8,128)(2,1)}, u32[]{:S(2)}) copy-start(bf16[1,2,256,1536]{3,2,1,0:T(8,128)(2,1)} %param.16) | copy-start | bytes 4718596
  7.2 149.3 %all-gather.5.cloned.1.call-start = ((), (), s32[]{:S(2)}) async-start(), calls=%async_computation.2 | async-start | bytes 14266368 | tf_op jit(solution)/shard_map/all_gather | solution.py:64
  9.0 267.2 %all-gather.7.cloned.1.call-start = ((), (), s32[]{:S(2)}) async-start(), calls=%async_computation.3 | async-start | bytes 4755456 | tf_op jit(solution)/shard_map/all_gather | solution.py:65
  18.2 147.2 %copy-start.24 = (bf16[1,2,24,1536]{3,2,1,0:T(8,128)(2,1)S(1)}, bf16[1,2,24,1536]{3,2,1,0:T(8,128)(2,1)}, u32[]{:S(2)}) copy-start(bf16[1,2,24,1536]{3,2,1,0:T(8,128)(2,1)} %param.17) | copy-start | bytes 442372
  171.6 40.4 %all-to-all-start = ((bf16[4,256,1536]{2,1,0:T(8,128)(2,1)}), bf16[4,256,1536]{2,1,0:T(8,128)(2,1)S(1)}, u32[]{:S(2)}, u32[]{:S(2)}) async-start(bf16[4,256,1536]{2,1,0:T(8,128)(2,1)} %bitcast.214), calls=%async_computation | async-start | bytes 6291456 | tf_op jit(solution)/shard_map/all_to_all | solution.py:13
  176.2 156.4 %copy-start.28 = (pred[1184]{0:T(1024)(128)(4,1)}, pred[1184]{0:T(1024)(128)(4,1)S(1)}, u32[]{:S(2)}) copy-start(pred[1184]{0:T(1024)(128)(4,1)S(1)} %concatenate.44) | copy-start | bytes 3556
  176.2 173.0 %copy-start.30 = (pred[1184]{0:T(1024)(128)(4,1)}, pred[1184]{0:T(1024)(128)(4,1)S(1)}, u32[]{:S(2)}) copy-start(pred[1184]{0:T(1024)(128)(4,1)S(1)} %concatenate.47) | copy-start | bytes 3556
  213.6 95.1 %all-to-all-start.1 = ((bf16[4,256,1536]{2,1,0:T(8,128)(2,1)}), bf16[4,256,1536]{2,1,0:T(8,128)(2,1)}, u32[]{:S(2)}, u32[]{:S(2)}) async-start(bf16[4,256,1536]{2,1,0:T(8,128)(2,1)} %bitcast.215), calls=%async_computation.1 | async-start | bytes 6291456 | tf_op jit(solution)/shard_map/all_to_all | solution.py:13
  358.6 13.4 %slice-start = ((s8[7077888]{0:T(1024)(128)(4,1)}), s8[4194304]{0:T(1024)(128)(4,1)S(1)}, s32[]{:S(2)}) async-start(s8[7077888]{0:T(1024)(128)(4,1)} %bitcast.220), calls=%async_computation.4 | async-start | bytes 8388608
  360.9 11.2 %slice-start.1 = ((s8[7077888]{0:T(1024)(128)(4,1)}), s8[2883584]{0:T(1024)(128)(4,1)S(1)}, s32[]{:S(2)}) async-start(s8[7077888]{0:T(1024)(128)(4,1)} %bitcast.220), calls=%async_computation.5 | async-start | bytes 5767168
  363.4 7.8 %collective-permute-start = (bf16[2,256,1536]{2,1,0:T(8,128)(2,1)S(1)}, bf16[2,256,1536]{2,1,0:T(8,128)(2,1)S(1)}, u32[]{:S(2)}, u32[]{:S(2)}) collective-permute-start(bf16[2,256,1536]{2,1,0:T(8,128)(2,1)S(1)} %pad_maximum_fusion.6), channel_id=1, source_target_pairs={{0,128},{1,129},{2,130},{3,131},{4,132},{5,133},{6,134},{7,135},{8... | collective-permute-start | bytes 4718600 | tf_op jit(solution)/shard_map/ppermute | solution.py:19
  371.1 4.4 copy-start.5
  377.7 4.6 %copy-start.18 = (bf16[256,2304]{1,0:T(8,128)(2,1)}, bf16[256,2304]{1,0:T(8,128)(2,1)S(1)}, u32[]{:S(2)}) copy-start(bf16[256,2304]{1,0:T(8,128)(2,1)S(1)} %convolution_convert_fusion.1) | copy-start | bytes 3538948
  382.3 4.0 slice-start.2
  386.5 12.3 %copy-start.26 = (bf16[256,768]{0,1:T(8,128)(2,1)}, bf16[256,768]{0,1:T(8,128)(2,1)S(1)}, u32[]{:S(2)}) copy-start(bf16[256,768]{0,1:T(8,128)(2,1)S(1)} %copy.62) | copy-start | bytes 1179652
  390.6 4.0 slice-start.3
  394.7 4.1 copy-start.31
  405.5 8.7 %copy-start.29 = (pred[1184]{0:T(1024)(128)(4,1)S(1)}, pred[1184]{0:T(1024)(128)(4,1)}, u32[]{:S(2)}) copy-start(pred[1184]{0:T(1024)(128)(4,1)} %copy-done.28) | copy-start | bytes 3556
  434.3 4.1 copy-start.27
  434.3 4.2 copy-start.13
  434.3 4.2 copy-start.14
  434.3 4.2 copy-start.15
  435.3 6.0 %collective-permute-start.1 = (bf16[2,256,768]{2,1,0:T(8,128)(2,1)}, bf16[2,256,768]{2,1,0:T(8,128)(2,1)}, u32[]{:S(2)}, u32[]{:S(2)}) collective-permute-start(bf16[2,256,768]{2,1,0:T(8,128)(2,1)} %fusion.94), channel_id=1, source_target_pairs={{128,0},{129,1},{130,2},{131,3},{132,4},{133,5},{134,6},{135,7},{1... | collective-permute-start | bytes 2359304 | tf_op jit(solution)/shard_map/ppermute | solution.py:19
  (19 other events, 41.2 us)
Sparse Core Ops, SparseCore 0:
  12.3 144.0 all-gather.4
  160.2 115.9 all-gather.6
